TPU v7x, 32 devices: a whole 2x2x4 slice. The times are simulated.
32 devices in a mesh: row: 4 (over y, x), col: 8 (over z, core).
Axes of the slice: x: 2, y: 2, z: 4, core: 2. Of those that a mesh axis runs over, the one named last changes fastest.
Arguments:
- frames: bfloat16 [4096, 440], P('col'), may hold values from -6 to 6
- center_picks: int32 [8, 8, 64], P('col'), may hold values from 0 to 511, as said below
- send_counts: int32 [8, 8], P(None, 'col'), may hold values from 0 to 64, as said below
- send_offsets: int32 [8, 8], P(None, 'col'), may hold values from 0 to 256, as said below
Outputs:
- factor_panels: float32 [4, 512, 1024], P('row', 'col')
- trailing: float32 [4, 512, 8, 256], P('row', None, 'col')
Inputs may be any that keep to these rules, and one draw needn't show every extreme that they name: `center_picks`: for each owner the entries over all destinations and slots are distinct local frame indices. `send_counts`: for each destination the counts over owners sum to 256; every destination has an owner that fills all 64 slots and one that sends nothing. `send_offsets`: for each destination the owners' segments [offset, offset + count) cover 0 to 255 without intersection, in an order that varies by destination; an owner that sends nothing may start at 256.
All inputs are finite; a program needn't handle non-finite values.
Results may differ from a plain program's by a relative error of at most 0.0003.
Values may be sent and summed in bfloat16 or wider, within the bound.
No kernel may reach another device: no remote copies, remote signals or barrier semaphores. Data moves between devices by JAX's collectives and lax.ppermute only.
A program may use at most 128 MiB of HBM per device.

v0:
```python
import jax
import jax.numpy as jnp
from jax import lax
from jax.sharding import PartitionSpec as P

PANEL = 256
PANELS = 4
CENT_DEV = 256
kernel_scale = 0.6
ridge_shift = 0.1


def spread(value, axis, source):
    kept = jnp.where(lax.axis_index(axis) == source, value, 0).astype(value.dtype)
    return lax.psum(kept, axis)


def gaussian(left_feats, right_feats):
    inner = lax.dot_general(
        left_feats, right_feats, (((1,), (1,)), ((), ())), preferred_element_type=jnp.float32
    )
    left_norm = jnp.sum(jnp.square(left_feats.astype(jnp.float32)), axis=1)
    right_norm = jnp.sum(jnp.square(right_feats.astype(jnp.float32)), axis=1)
    feat_width = left_feats.shape[1]
    return jnp.exp(
        -(kernel_scale / feat_width) * (left_norm[:, None] + right_norm[None, :] - 2.0 * inner)
    )


def outer_minus(column, panel_cols, rows_piece):
    return column - lax.dot_general(
        panel_cols,
        rows_piece,
        (((1,), (1,)), ((), ())),
        precision=lax.Precision.HIGHEST,
        preferred_element_type=jnp.float32,
    )


def make_panel(column, factor, row_tile, panel_step):
    solved = jax.scipy.linalg.solve_triangular(factor, column.T, lower=True).T
    repeated = jnp.tile(factor, (column.shape[0] // factor.shape[0], 1))
    return jnp.where(
        (row_tile > panel_step)[:, None],
        solved,
        jnp.where((row_tile == panel_step)[:, None], repeated, jnp.zeros_like(solved)),
    )


def update_slots(columns, panel_cols, col_rows):
    columns[0] = outer_minus(columns[0], panel_cols, col_rows)
    return columns


def per_device(frames, center_picks, send_counts, send_offsets):
    rows_axis = lax.axis_size("row")
    cols_axis = lax.axis_size("col")
    row_id = lax.axis_index("row")
    col_id = lax.axis_index("col")
    feat_width = frames.shape[1]
    capacity = center_picks.shape[2]
    outgoing = frames[center_picks[0]]
    incoming = lax.all_to_all(outgoing, "col", split_axis=0, concat_axis=0, tiled=True)
    position = jnp.arange(CENT_DEV, dtype=jnp.int32)
    starts = send_offsets[:, 0]
    lengths = send_counts[:, 0]
    inside = (position[:, None] >= starts[None, :]) & (
        position[:, None] < (starts + lengths)[None, :]
    )
    source = jnp.sum(jnp.where(inside, jnp.arange(cols_axis, dtype=jnp.int32)[None, :], 0), axis=1)
    within = position - jnp.sum(jnp.where(inside, starts[None, :], 0), axis=1)
    own_feats = incoming.reshape(cols_axis * capacity, feat_width)[source * capacity + within]
    col_slots = CENT_DEV // PANEL
    row_tiles_dev = col_slots * cols_axis // rows_axis
    rows_dev = row_tiles_dev * PANEL
    tile_range = jnp.arange(row_tiles_dev, dtype=jnp.int32)
    gathered = lax.all_gather(own_feats, "col", axis=0, tiled=True)
    blocks = gathered.reshape(cols_axis, col_slots, PANEL, feat_width)
    my_tiles = row_id + rows_axis * tile_range
    row_feats = blocks[my_tiles % cols_axis, my_tiles // cols_axis].reshape(rows_dev, feat_width)
    local_rows = jnp.arange(rows_dev, dtype=jnp.int32)
    row_tile = row_id + rows_axis * (local_rows // PANEL)
    global_row = row_tile * PANEL + local_rows % PANEL
    local_cols = jnp.arange(CENT_DEV, dtype=jnp.int32)
    global_col = (col_id + cols_axis * (local_cols // PANEL)) * PANEL + local_cols % PANEL
    kernel = gaussian(row_feats, own_feats) + ridge_shift * (
        global_row[:, None] == global_col[None, :]
    ).astype(jnp.float32)
    columns = [kernel]
    panels = []
    for panel_step in range(PANELS):
        slot_now = panel_step // cols_axis
        tile_slot = panel_step // rows_axis
        diag_here = columns[slot_now][tile_slot * PANEL : (tile_slot + 1) * PANEL]
        diag_block = spread(diag_here, "row", panel_step % rows_axis)
        factor = jnp.linalg.cholesky(diag_block)
        panel_here = make_panel(columns[slot_now], factor, row_tile, panel_step)
        panel_cols = spread(panel_here, "col", panel_step % cols_axis)
        here_rows = lax.dynamic_slice_in_dim(
            panel_cols, (col_id + 0) // rows_axis * PANEL, PANEL, 0
        )
        col_rows = spread(here_rows, "row", col_id % rows_axis)
        panels.append(panel_cols)
        columns = update_slots(columns, panel_cols, col_rows)
    trailing = columns[0].reshape(1, rows_dev, 1, CENT_DEV)
    every_panel = jnp.concatenate(panels, axis=1)
    share_rows = rows_dev // cols_axis
    panel_share = lax.dynamic_slice_in_dim(every_panel, col_id * share_rows, share_rows, 0).reshape(
        1, share_rows, PANELS * PANEL
    )
    return (panel_share, trailing)


def solution(mesh):
    in_specs = (P("col", None), P("col", None, None), P(None, "col"), P(None, "col"))
    out_specs = (P("row", "col", None), P("row", None, "col", None))
    return jax.shard_map(
        per_device, mesh=mesh, in_specs=in_specs, out_specs=out_specs, check_vma=False
    )
```

profile of v0, /device:TPU:0, one launch (start us, length us, event | category | flops | bytes accessed | tf_op | source)
XLA Modules:
  0.0 926.6 jit_solution(15417714206202597751)
XLA Ops:
  11.8 6.3 all-to-all-start
  18.3 15.2 %all-to-all-done = bf16[8,64,440]{2,1,0:T(8,128)(2,1)S(1)} async-done(((bf16[8,64,440]{2,1,0:T(8,128)(2,1)}), bf16[8,64,440]{2,1,0:T(8,128)(2,1)S(1)}, u32[]{:S(2)}, u32[]{:S(2)}) %all-to-all-start) | async-done | bytes 450592 | tf_op jit(solution)/shard_map/all_to_all | solution.py:63
  36.6 27.0 %all-gather.3.cloned.1.call-done = bf16[2048,440]{1,0:T(8,128)(2,1)} async-done(((bf16[256,440]{1,0:T(8,128)(2,1)}), bf16[2048,440]{1,0:T(8,128)(2,1)}) %all-gather.3.cloned.1.call-update) | async-done | bytes 1802256 | tf_op jit(solution)/shard_map/all_gather | solution.py:77
  67.6 42.3 %all-reduce.14.cloned.1.call-done = f32[256,256]{0,1:T(8,128)} async-done(((f32[256,256]{0,1:T(8,128)}), f32[256,256]{0,1:T(8,128)}) %all-reduce.14.cloned.1.call-update) | async-done | bytes 262160 | tf_op jit(solution)/shard_map/psum | solution.py:15
  112.0 11.7 %cholesky.214 = f32[128,128]{1,0:T(8,128)S(1)} custom-call(f32[128,128]{1,0:T(8,128)S(1)} %cholesky.346), custom_call_target="Cholesky" | custom-call | tf_op jit(solution)/shard_map/jit(cholesky)/cholesky | solution.py:96
  123.7 9.8 %custom-call.19 = f32[1,128,128]{1,2,0:T(8,128)S(1)} custom-call(f32[1,128,128]{2,1,0:T(8,128)S(1)} %get-tuple-element.105), custom_call_target="InvertDiagBlocksLowerTriangular" | custom-call | tf_op jit(solution)/shard_map/jit(cholesky)/cholesky | solution.py:96
  134.0 11.7 %cholesky.231 = f32[128,128]{1,0:T(8,128)S(1)} custom-call(f32[128,128]{1,0:T(8,128)S(1)} %convolution_subtract_fusion.8), custom_call_target="Cholesky" | custom-call | tf_op jit(solution)/shard_map/jit(cholesky)/cholesky | solution.py:96
  148.0 4.6 while.8
  152.6 19.7 %custom-call.20 = f32[2,128,128]{1,2,0:T(8,128)S(1)} custom-call(f32[2,128,128]{2,1,0:T(8,128)S(1)} %get-tuple-element.30), custom_call_target="InvertDiagBlocksLowerTriangular" | custom-call | tf_op jit(solution)/shard_map/jit(_solve_triangular)/triangular_solve | solution.py:41
  174.8 56.2 %all-reduce.16.cloned.1.call-done = f32[512,256]{0,1:T(8,128)} async-done(((f32[512,256]{0,1:T(8,128)}), f32[512,256]{0,1:T(8,128)}) %all-reduce.16.cloned.1.call-update) | async-done | bytes 524304 | tf_op jit(solution)/shard_map/psum | solution.py:15
  232.8 43.5 %all-reduce.18.cloned.1.call-done = f32[256,256]{0,1:T(8,128)} async-done(((f32[256,256]{0,1:T(8,128)}), f32[256,256]{0,1:T(8,128)}) %all-reduce.18.cloned.1.call-update) | async-done | bytes 262160 | tf_op jit(solution)/shard_map/psum | solution.py:15
  279.2 43.7 %all-reduce.20.cloned.1.call-done = f32[256,256]{0,1:T(8,128)} async-done(((f32[256,256]{0,1:T(8,128)}), f32[256,256]{0,1:T(8,128)}) %all-reduce.20.cloned.1.call-update) | async-done | bytes 262160 | tf_op jit(solution)/shard_map/psum | solution.py:15
  325.0 11.7 %cholesky.248 = f32[128,128]{1,0:T(8,128)S(1)} custom-call(f32[128,128]{1,0:T(8,128)S(1)} %cholesky.349), custom_call_target="Cholesky" | custom-call | tf_op jit(solution)/shard_map/jit(cholesky)/cholesky | solution.py:96
  336.8 9.8 %custom-call.21 = f32[1,128,128]{1,2,0:T(8,128)S(1)} custom-call(f32[1,128,128]{2,1,0:T(8,128)S(1)} %get-tuple-element.101), custom_call_target="InvertDiagBlocksLowerTriangular" | custom-call | tf_op jit(solution)/shard_map/jit(cholesky)/cholesky | solution.py:96
  347.1 11.7 %cholesky.265 = f32[128,128]{1,0:T(8,128)S(1)} custom-call(f32[128,128]{1,0:T(8,128)S(1)} %convolution_subtract_fusion.7), custom_call_target="Cholesky" | custom-call | tf_op jit(solution)/shard_map/jit(cholesky)/cholesky | solution.py:96
  365.9 19.7 %custom-call.22 = f32[2,128,128]{1,2,0:T(8,128)S(1)} custom-call(f32[2,128,128]{2,1,0:T(8,128)S(1)} %get-tuple-element.31), custom_call_target="InvertDiagBlocksLowerTriangular" | custom-call | tf_op jit(solution)/shard_map/jit(_solve_triangular)/triangular_solve | solution.py:41
  388.1 56.3 %all-reduce.22.cloned.1.call-done = f32[512,256]{0,1:T(8,128)} async-done(((f32[512,256]{0,1:T(8,128)}), f32[512,256]{0,1:T(8,128)}) %all-reduce.22.cloned.1.call-update) | async-done | bytes 524304 | tf_op jit(solution)/shard_map/psum | solution.py:15
  446.2 43.9 %all-reduce.24.cloned.1.call-done = f32[256,256]{0,1:T(8,128)} async-done(((f32[256,256]{0,1:T(8,128)}), f32[256,256]{0,1:T(8,128)}) %all-reduce.24.cloned.1.call-update) | async-done | bytes 262160 | tf_op jit(solution)/shard_map/psum | solution.py:15
  492.8 43.8 %all-reduce.26.cloned.1.call-done = f32[256,256]{0,1:T(8,128)} async-done(((f32[256,256]{0,1:T(8,128)}), f32[256,256]{0,1:T(8,128)}) %all-reduce.26.cloned.1.call-update) | async-done | bytes 262160 | tf_op jit(solution)/shard_map/psum | solution.py:15
  538.6 11.7 %cholesky.282 = f32[128,128]{1,0:T(8,128)S(1)} custom-call(f32[128,128]{1,0:T(8,128)S(1)} %cholesky.352), custom_call_target="Cholesky" | custom-call | tf_op jit(solution)/shard_map/jit(cholesky)/cholesky | solution.py:96
  550.4 9.8 %custom-call.23 = f32[1,128,128]{1,2,0:T(8,128)S(1)} custom-call(f32[1,128,128]{2,1,0:T(8,128)S(1)} %get-tuple-element.97), custom_call_target="InvertDiagBlocksLowerTriangular" | custom-call | tf_op jit(solution)/shard_map/jit(cholesky)/cholesky | solution.py:96
  560.7 11.7 %cholesky.299 = f32[128,128]{1,0:T(8,128)S(1)} custom-call(f32[128,128]{1,0:T(8,128)S(1)} %convolution_subtract_fusion.6), custom_call_target="Cholesky" | custom-call | tf_op jit(solution)/shard_map/jit(cholesky)/cholesky | solution.py:96
  579.5 19.7 %custom-call.24 = f32[2,128,128]{1,2,0:T(8,128)S(1)} custom-call(f32[2,128,128]{2,1,0:T(8,128)S(1)} %get-tuple-element.32), custom_call_target="InvertDiagBlocksLowerTriangular" | custom-call | tf_op jit(solution)/shard_map/jit(_solve_triangular)/triangular_solve | solution.py:41
  601.8 56.3 %all-reduce.28.cloned.1.call-done = f32[512,256]{0,1:T(8,128)} async-done(((f32[512,256]{0,1:T(8,128)}), f32[512,256]{0,1:T(8,128)}) %all-reduce.28.cloned.1.call-update) | async-done | bytes 524304 | tf_op jit(solution)/shard_map/psum | solution.py:15
  659.8 43.5 %all-reduce.30.cloned.1.call-done = f32[256,256]{0,1:T(8,128)} async-done(((f32[256,256]{0,1:T(8,128)}), f32[256,256]{0,1:T(8,128)}) %all-reduce.30.cloned.1.call-update) | async-done | bytes 262160 | tf_op jit(solution)/shard_map/psum | solution.py:15
  706.0 44.0 %all-reduce.32.cloned.1.call-done = f32[256,256]{0,1:T(8,128)} async-done(((f32[256,256]{0,1:T(8,128)}), f32[256,256]{0,1:T(8,128)}) %all-reduce.32.cloned.1.call-update) | async-done | bytes 262160 | tf_op jit(solution)/shard_map/psum | solution.py:15
  752.1 11.7 %cholesky.316 = f32[128,128]{1,0:T(8,128)S(1)} custom-call(f32[128,128]{1,0:T(8,128)S(1)} %cholesky.355), custom_call_target="Cholesky" | custom-call | tf_op jit(solution)/shard_map/jit(cholesky)/cholesky | solution.py:96
  763.9 9.8 %custom-call.25 = f32[1,128,128]{1,2,0:T(8,128)S(1)} custom-call(f32[1,128,128]{2,1,0:T(8,128)S(1)} %get-tuple-element.93), custom_call_target="InvertDiagBlocksLowerTriangular" | custom-call | tf_op jit(solution)/shard_map/jit(cholesky)/cholesky | solution.py:96
  774.2 11.7 %cholesky.333 = f32[128,128]{1,0:T(8,128)S(1)} custom-call(f32[128,128]{1,0:T(8,128)S(1)} %convolution_subtract_fusion.5), custom_call_target="Cholesky" | custom-call | tf_op jit(solution)/shard_map/jit(cholesky)/cholesky | solution.py:96
  792.8 19.7 %custom-call.26 = f32[2,128,128]{1,2,0:T(8,128)S(1)} custom-call(f32[2,128,128]{2,1,0:T(8,128)S(1)} %get-tuple-element.33), custom_call_target="InvertDiagBlocksLowerTriangular" | custom-call | tf_op jit(solution)/shard_map/jit(_solve_triangular)/triangular_solve | solution.py:41
  815.1 56.3 %all-reduce.34.cloned.1.call-done = f32[512,256]{0,1:T(8,128)} async-done(((f32[512,256]{0,1:T(8,128)}), f32[512,256]{0,1:T(8,128)}) %all-reduce.34.cloned.1.call-update) | async-done | bytes 524304 | tf_op jit(solution)/shard_map/psum | solution.py:15
  875.1 41.9 %all-reduce.36.cloned.1.call-done = f32[256,256]{0,1:T(8,128)} async-done(((f32[256,256]{0,1:T(8,128)}), f32[256,256]{0,1:T(8,128)}) %all-reduce.36.cloned.1.call-update) | async-done | bytes 262160 | tf_op jit(solution)/shard_map/psum | solution.py:15
  (186 shorter events, 85.8 us)
Async XLA Ops:
  9.2 9.0 copy-start.5
  9.2 9.0 copy-start.6
  11.8 21.7 %all-to-all-start = ((bf16[8,64,440]{2,1,0:T(8,128)(2,1)}), bf16[8,64,440]{2,1,0:T(8,128)(2,1)S(1)}, u32[]{:S(2)}, u32[]{:S(2)}) async-start(bf16[8,64,440]{2,1,0:T(8,128)(2,1)} %bitcast.1), calls=%async_computation | async-start | bytes 1048576 | tf_op jit(solution)/shard_map/all_to_all | solution.py:63
  18.1 45.4 %all-gather.3.cloned.1.call-start = ((), (), s32[]{:S(2)}) async-start(), calls=%async_computation.13 | async-start | bytes 2359296 | tf_op jit(solution)/shard_map/all_gather | solution.py:77
  35.3 30.6 %copy-start.4 = (bf16[256,440]{1,0:T(8,128)(2,1)S(1)}, bf16[256,440]{1,0:T(8,128)(2,1)}, u32[]{:S(2)}) copy-start(bf16[256,440]{1,0:T(8,128)(2,1)} %gather_fusion.1) | copy-start | bytes 675844
  35.4 74.5 %all-reduce.14.cloned.1.call-start = ((), (), s32[]{:S(2)}) async-start(), calls=%async_computation.1 | async-start | bytes 524288 | tf_op jit(solution)/shard_map/psum | solution.py:15
  67.3 163.8 %all-reduce.16.cloned.1.call-start = ((), (), s32[]{:S(2)}) async-start(), calls=%async_computation.2 | async-start | bytes 1048576 | tf_op jit(solution)/shard_map/psum | solution.py:15
  174.8 101.6 %all-reduce.18.cloned.1.call-start = ((), (), s32[]{:S(2)}) async-start(), calls=%async_computation.3 | async-start | bytes 524288 | tf_op jit(solution)/shard_map/psum | solution.py:15
  232.8 90.2 %all-reduce.20.cloned.1.call-start = ((), (), s32[]{:S(2)}) async-start(), calls=%async_computation.4 | async-start | bytes 524288 | tf_op jit(solution)/shard_map/psum | solution.py:15
  279.1 165.3 %all-reduce.22.cloned.1.call-start = ((), (), s32[]{:S(2)}) async-start(), calls=%async_computation.5 | async-start | bytes 1048576 | tf_op jit(solution)/shard_map/psum | solution.py:15
  388.1 102.0 %all-reduce.24.cloned.1.call-start = ((), (), s32[]{:S(2)}) async-start(), calls=%async_computation.6 | async-start | bytes 524288 | tf_op jit(solution)/shard_map/psum | solution.py:15
  446.1 90.5 %all-reduce.26.cloned.1.call-start = ((), (), s32[]{:S(2)}) async-start(), calls=%async_computation.7 | async-start | bytes 524288 | tf_op jit(solution)/shard_map/psum | solution.py:15
  492.7 165.4 %all-reduce.28.cloned.1.call-start = ((), (), s32[]{:S(2)}) async-start(), calls=%async_computation.8 | async-start | bytes 1048576 | tf_op jit(solution)/shard_map/psum | solution.py:15
  601.7 101.6 %all-reduce.30.cloned.1.call-start = ((), (), s32[]{:S(2)}) async-start(), calls=%async_computation.9 | async-start | bytes 524288 | tf_op jit(solution)/shard_map/psum | solution.py:15
  659.8 90.3 %all-reduce.32.cloned.1.call-start = ((), (), s32[]{:S(2)}) async-start(), calls=%async_computation.10 | async-start | bytes 524288 | tf_op jit(solution)/shard_map/psum | solution.py:15
  706.0 165.4 %all-reduce.34.cloned.1.call-start = ((), (), s32[]{:S(2)}) async-start(), calls=%async_computation.11 | async-start | bytes 1048576 | tf_op jit(solution)/shard_map/psum | solution.py:15
  814.0 59.1 %copy-start.1 = (f32[512,256]{0,1:T(8,128)S(1)}, f32[512,256]{0,1:T(8,128)}, u32[]{:S(2)}) copy-start(f32[512,256]{0,1:T(8,128)} %all-reduce.16.cloned.1.call-done) | copy-start | bytes 1572868
  814.0 59.1 %copy-start.2 = (f32[512,256]{0,1:T(8,128)S(1)}, f32[512,256]{0,1:T(8,128)}, u32[]{:S(2)}) copy-start(f32[512,256]{0,1:T(8,128)} %all-reduce.22.cloned.1.call-done) | copy-start | bytes 1572868
  814.0 59.1 %copy-start.3 = (f32[512,256]{0,1:T(8,128)S(1)}, f32[512,256]{0,1:T(8,128)}, u32[]{:S(2)}) copy-start(f32[512,256]{0,1:T(8,128)} %all-reduce.28.cloned.1.call-done) | copy-start | bytes 1572868
  815.0 102.0 %all-reduce.36.cloned.1.call-start = ((), (), s32[]{:S(2)}) async-start(), calls=%async_computation.12 | async-start | bytes 524288 | tf_op jit(solution)/shard_map/psum | solution.py:15
  871.3 45.7 %copy-start = (f32[512,256]{0,1:T(8,128)S(1)}, f32[512,256]{0,1:T(8,128)}, u32[]{:S(2)}) copy-start(f32[512,256]{0,1:T(8,128)} %all-reduce.34.cloned.1.call-done) | copy-start | bytes 1572868
Sparse Core Ops, SparseCore 0:
  35.5 27.9 all-gather.2
  67.4 42.4 all-reduce.13
  174.9 56.1 all-reduce.15
  234.4 41.8 all-reduce.17
  280.0 42.9 all-reduce.19
  388.2 56.1 all-reduce.21
  448.2 41.8 all-reduce.23
  493.6 42.9 all-reduce.25
  601.9 56.1 all-reduce.27
  661.4 41.9 all-reduce.29
  707.1 42.9 all-reduce.31
  815.1 56.1 all-reduce.33
  875.1 41.8 all-reduce.35
where the time goes:
time: 930 us; the launch traced here: 927 us
  waiting for transfers between devices  614 us (66%)
  other arithmetic  238 us (26%)
  local copies, waits for them, and re-layouts  31.9 us (3%)
  between operations  20.4 us (2%)
  matrix products  14 us (2%)
    psum x12, waiting for transfers between devices, spread(): return lax.psum(kept, axis)  572 us
    another operation x27, other arithmetic, per_device(): factor = jnp.linalg.cholesky(diag_block)  138 us
    another operation x9, other arithmetic, make_panel(): solved = jax.scipy.linalg.solve_triangular(factor, column.T, lower=True).T  78.8 us
    all_gather x1, waiting for transfers between devices, per_device(): gathered = lax.all_gather(own_feats, 'col', axis=0, tiled=True)  27 us
  transfers between devices with their start and end apart: 14, of which 14 were waited for; matrix products, arithmetic and copies ran while one was open for 0% of the time, Pallas kernels for 0%

commit v1 on v0

--- a/solution.py
+++ b/solution.py
@@ -12,7 +12,7 @@
 
 def spread(value, axis, source):
     kept = jnp.where(lax.axis_index(axis) == source, value, 0).astype(value.dtype)
-    return lax.psum(kept, axis)
+    return jnp.sum(lax.all_gather(kept, axis), axis=0)
 
 
 def gaussian(left_feats, right_feats):

time: 930 us -> 761 us (0.82)
  waiting for transfers between devices: 614 us -> 438 us
  other arithmetic: 238 us -> 253 us
    psum x12 -> x0, waiting for transfers between devices: 572 us -> none  [spread(): return lax.psum(kept, axis)]
    all_gather x0 -> x12, waiting for transfers between devices: none -> 396 us  [spread(): return jnp.sum(lax.all_gather(kept, axis), axis=0)]
    reduce_sum x0 -> x12, other arithmetic: none -> 20.6 us  [spread(): return jnp.sum(lax.all_gather(kept, axis), axis=0)]
where the time goes in v1:
time: 761 us; the launch traced here: 758 us
  waiting for transfers between devices  438 us (58%)
  other arithmetic  253 us (33%)
  local copies, waits for them, and re-layouts  26.7 us (4%)
  between operations  20.2 us (3%)
  matrix products  11 us (1%)
    all_gather x12, waiting for transfers between devices, spread(): return jnp.sum(lax.all_gather(kept, axis), axis=0)  396 us
    another operation x27, other arithmetic, per_device(): factor = jnp.linalg.cholesky(diag_block)  138 us
    another operation x9, other arithmetic, make_panel(): solved = jax.scipy.linalg.solve_triangular(factor, column.T, lower=True).T  79.6 us
    all_gather x1, waiting for transfers between devices, per_device(): gathered = lax.all_gather(own_feats, 'col', axis=0, tiled=True)  27 us
    reduce_sum x12, other arithmetic, spread(): return jnp.sum(lax.all_gather(kept, axis), axis=0)  20.6 us
    another operation x33, local copies, waits for them, and re-layouts, make_panel(): solved = jax.scipy.linalg.solve_triangular(factor, column.T, lower=True).T  16.8 us
  transfers between devices with their start and end apart: 14, of which 14 were waited for; matrix products, arithmetic and copies ran while one was open for 0% of the time, Pallas kernels for 0%

profile of v1, /device:TPU:0, one launch (start us, length us, event | category | flops | bytes accessed | tf_op | source)
XLA Modules:
  0.0 757.6 jit_solution(11719426082781270576)
XLA Ops:
  11.8 6.3 all-to-all-start
  18.3 15.2 %all-to-all-done = bf16[8,64,440]{2,1,0:T(8,128)(2,1)S(1)} async-done(((bf16[8,64,440]{2,1,0:T(8,128)(2,1)}), bf16[8,64,440]{2,1,0:T(8,128)(2,1)S(1)}, u32[]{:S(2)}, u32[]{:S(2)}) %all-to-all-start) | async-done | bytes 450592 | tf_op jit(solution)/shard_map/all_to_all | solution.py:63
  36.6 27.0 %all-gather.27.cloned.1.call-done = bf16[2048,440]{1,0:T(8,128)(2,1)} async-done(((bf16[256,440]{1,0:T(8,128)(2,1)}), bf16[2048,440]{1,0:T(8,128)(2,1)}) %all-gather.27.cloned.1.call-update) | async-done | bytes 1802256 | tf_op jit(solution)/shard_map/all_gather | solution.py:77
  67.6 25.9 %all-gather.29.cloned.1.call-done = f32[1024,256]{1,0:T(8,128)} async-done(((f32[256,256]{1,0:T(8,128)}), f32[1024,256]{1,0:T(8,128)}) %all-gather.29.cloned.1.call-update) | async-done | bytes 1048592 | tf_op jit(solution)/shard_map/all_gather | solution.py:15
  95.1 11.7 %cholesky.214 = f32[128,128]{1,0:T(8,128)S(1)} custom-call(f32[128,128]{1,0:T(8,128)S(1)} %cholesky.346), custom_call_target="Cholesky" | custom-call | tf_op jit(solution)/shard_map/jit(cholesky)/cholesky | solution.py:96
  106.8 9.8 %custom-call.19 = f32[1,128,128]{1,2,0:T(8,128)S(1)} custom-call(f32[1,128,128]{2,1,0:T(8,128)S(1)} %get-tuple-element.107), custom_call_target="InvertDiagBlocksLowerTriangular" | custom-call | tf_op jit(solution)/shard_map/jit(cholesky)/cholesky | solution.py:96
  117.1 11.7 %cholesky.231 = f32[128,128]{1,0:T(8,128)S(1)} custom-call(f32[128,128]{1,0:T(8,128)S(1)} %convolution_subtract_fusion.8), custom_call_target="Cholesky" | custom-call | tf_op jit(solution)/shard_map/jit(cholesky)/cholesky | solution.py:96
  131.1 4.7 while.8
  135.8 19.7 %custom-call.20 = f32[2,128,128]{1,2,0:T(8,128)S(1)} custom-call(f32[2,128,128]{2,1,0:T(8,128)S(1)} %get-tuple-element.30), custom_call_target="InvertDiagBlocksLowerTriangular" | custom-call | tf_op jit(solution)/shard_map/jit(_solve_triangular)/triangular_solve | solution.py:41
  158.1 47.2 %all-gather.31.cloned.1.call-done = f32[4096,256]{1,0:T(8,128)} async-done(((f32[512,256]{1,0:T(8,128)}), f32[4096,256]{1,0:T(8,128)}) %all-gather.31.cloned.1.call-update) | async-done | bytes 4194320 | tf_op jit(solution)/shard_map/all_gather | solution.py:15
  208.6 25.4 %all-gather.33.cloned.1.call-done = f32[1024,256]{1,0:T(8,128)} async-done(((f32[256,256]{1,0:T(8,128)}), f32[1024,256]{1,0:T(8,128)}) %all-gather.33.cloned.1.call-update) | async-done | bytes 1048592 | tf_op jit(solution)/shard_map/all_gather | solution.py:15
  237.1 26.7 %all-gather.35.cloned.1.call-done = f32[1024,256]{1,0:T(8,128)} async-done(((f32[256,256]{1,0:T(8,128)}), f32[1024,256]{1,0:T(8,128)}) %all-gather.35.cloned.1.call-update) | async-done | bytes 1048592 | tf_op jit(solution)/shard_map/all_gather | solution.py:15
  265.3 11.7 %cholesky.248 = f32[128,128]{1,0:T(8,128)S(1)} custom-call(f32[128,128]{1,0:T(8,128)S(1)} %cholesky.349), custom_call_target="Cholesky" | custom-call | tf_op jit(solution)/shard_map/jit(cholesky)/cholesky | solution.py:96
  277.1 9.8 %custom-call.21 = f32[1,128,128]{1,2,0:T(8,128)S(1)} custom-call(f32[1,128,128]{2,1,0:T(8,128)S(1)} %get-tuple-element.103), custom_call_target="InvertDiagBlocksLowerTriangular" | custom-call | tf_op jit(solution)/shard_map/jit(cholesky)/cholesky | solution.py:96
  287.4 11.7 %cholesky.265 = f32[128,128]{1,0:T(8,128)S(1)} custom-call(f32[128,128]{1,0:T(8,128)S(1)} %convolution_subtract_fusion.7), custom_call_target="Cholesky" | custom-call | tf_op jit(solution)/shard_map/jit(cholesky)/cholesky | solution.py:96
  306.2 19.7 %custom-call.22 = f32[2,128,128]{1,2,0:T(8,128)S(1)} custom-call(f32[2,128,128]{2,1,0:T(8,128)S(1)} %get-tuple-element.31), custom_call_target="InvertDiagBlocksLowerTriangular" | custom-call | tf_op jit(solution)/shard_map/jit(_solve_triangular)/triangular_solve | solution.py:41
  328.5 47.2 %all-gather.37.cloned.1.call-done = f32[4096,256]{1,0:T(8,128)} async-done(((f32[512,256]{1,0:T(8,128)}), f32[4096,256]{1,0:T(8,128)}) %all-gather.37.cloned.1.call-update) | async-done | bytes 4194320 | tf_op jit(solution)/shard_map/all_gather | solution.py:15
  379.0 25.4 %all-gather.39.cloned.1.call-done = f32[1024,256]{1,0:T(8,128)} async-done(((f32[256,256]{1,0:T(8,128)}), f32[1024,256]{1,0:T(8,128)}) %all-gather.39.cloned.1.call-update) | async-done | bytes 1048592 | tf_op jit(solution)/shard_map/all_gather | solution.py:15
  407.3 26.7 %all-gather.41.cloned.1.call-done = f32[1024,256]{1,0:T(8,128)} async-done(((f32[256,256]{1,0:T(8,128)}), f32[1024,256]{1,0:T(8,128)}) %all-gather.41.cloned.1.call-update) | async-done | bytes 1048592 | tf_op jit(solution)/shard_map/all_gather | solution.py:15
  435.6 11.7 %cholesky.282 = f32[128,128]{1,0:T(8,128)S(1)} custom-call(f32[128,128]{1,0:T(8,128)S(1)} %cholesky.352), custom_call_target="Cholesky" | custom-call | tf_op jit(solution)/shard_map/jit(cholesky)/cholesky | solution.py:96
  447.3 9.8 %custom-call.23 = f32[1,128,128]{1,2,0:T(8,128)S(1)} custom-call(f32[1,128,128]{2,1,0:T(8,128)S(1)} %get-tuple-element.99), custom_call_target="InvertDiagBlocksLowerTriangular" | custom-call | tf_op jit(solution)/shard_map/jit(cholesky)/cholesky | solution.py:96
  457.6 11.7 %cholesky.299 = f32[128,128]{1,0:T(8,128)S(1)} custom-call(f32[128,128]{1,0:T(8,128)S(1)} %convolution_subtract_fusion.6), custom_call_target="Cholesky" | custom-call | tf_op jit(solution)/shard_map/jit(cholesky)/cholesky | solution.py:96
  476.7 19.7 %custom-call.24 = f32[2,128,128]{1,2,0:T(8,128)S(1)} custom-call(f32[2,128,128]{2,1,0:T(8,128)S(1)} %get-tuple-element.32), custom_call_target="InvertDiagBlocksLowerTriangular" | custom-call | tf_op jit(solution)/shard_map/jit(_solve_triangular)/triangular_solve | solution.py:41
  498.9 47.3 %all-gather.43.cloned.1.call-done = f32[4096,256]{1,0:T(8,128)} async-done(((f32[512,256]{1,0:T(8,128)}), f32[4096,256]{1,0:T(8,128)}) %all-gather.43.cloned.1.call-update) | async-done | bytes 4194320 | tf_op jit(solution)/shard_map/all_gather | solution.py:15
  549.5 25.4 %all-gather.45.cloned.1.call-done = f32[1024,256]{1,0:T(8,128)} async-done(((f32[256,256]{1,0:T(8,128)}), f32[1024,256]{1,0:T(8,128)}) %all-gather.45.cloned.1.call-update) | async-done | bytes 1048592 | tf_op jit(solution)/shard_map/all_gather | solution.py:15
  578.6 26.7 %all-gather.47.cloned.1.call-done = f32[1024,256]{1,0:T(8,128)} async-done(((f32[256,256]{1,0:T(8,128)}), f32[1024,256]{1,0:T(8,128)}) %all-gather.47.cloned.1.call-update) | async-done | bytes 1048592 | tf_op jit(solution)/shard_map/all_gather | solution.py:15
  606.8 11.7 %cholesky.316 = f32[128,128]{1,0:T(8,128)S(1)} custom-call(f32[128,128]{1,0:T(8,128)S(1)} %cholesky.355), custom_call_target="Cholesky" | custom-call | tf_op jit(solution)/shard_map/jit(cholesky)/cholesky | solution.py:96
  618.6 9.8 %custom-call.25 = f32[1,128,128]{1,2,0:T(8,128)S(1)} custom-call(f32[1,128,128]{2,1,0:T(8,128)S(1)} %get-tuple-element.95), custom_call_target="InvertDiagBlocksLowerTriangular" | custom-call | tf_op jit(solution)/shard_map/jit(cholesky)/cholesky | solution.py:96
  628.9 11.7 %cholesky.333 = f32[128,128]{1,0:T(8,128)S(1)} custom-call(f32[128,128]{1,0:T(8,128)S(1)} %convolution_subtract_fusion.5), custom_call_target="Cholesky" | custom-call | tf_op jit(solution)/shard_map/jit(cholesky)/cholesky | solution.py:96
  648.3 19.7 %custom-call.26 = f32[2,128,128]{1,2,0:T(8,128)S(1)} custom-call(f32[2,128,128]{2,1,0:T(8,128)S(1)} %get-tuple-element.33), custom_call_target="InvertDiagBlocksLowerTriangular" | custom-call | tf_op jit(solution)/shard_map/jit(_solve_triangular)/triangular_solve | solution.py:41
  671.6 47.2 %all-gather.49.cloned.1.call-done = f32[4096,256]{1,0:T(8,128)} async-done(((f32[512,256]{1,0:T(8,128)}), f32[4096,256]{1,0:T(8,128)}) %all-gather.49.cloned.1.call-update) | async-done | bytes 4194320 | tf_op jit(solution)/shard_map/all_gather | solution.py:15
  722.8 24.8 %all-gather.51.cloned.1.call-done = f32[1024,256]{1,0:T(8,128)} async-done(((f32[256,256]{1,0:T(8,128)}), f32[1024,256]{1,0:T(8,128)}) %all-gather.51.cloned.1.call-update) | async-done | bytes 1048592 | tf_op jit(solution)/shard_map/all_gather | solution.py:15
  (183 shorter events, 92.7 us)
Async XLA Ops:
  9.2 9.0 %copy-start.2 = (s32[8,1]{0,1:T(1,128)S(1)}, s32[8,1]{0,1:T(1,128)}, u32[]{:S(2)}) copy-start(s32[8,1]{0,1:T(1,128)} %param.10) | copy-start | bytes 100
  9.2 9.0 %copy-start.3 = (s32[8,1]{0,1:T(1,128)S(1)}, s32[8,1]{0,1:T(1,128)}, u32[]{:S(2)}) copy-start(s32[8,1]{0,1:T(1,128)} %param.9) | copy-start | bytes 100
  11.8 21.7 %all-to-all-start = ((bf16[8,64,440]{2,1,0:T(8,128)(2,1)}), bf16[8,64,440]{2,1,0:T(8,128)(2,1)S(1)}, u32[]{:S(2)}, u32[]{:S(2)}) async-start(bf16[8,64,440]{2,1,0:T(8,128)(2,1)} %bitcast.1), calls=%async_computation | async-start | bytes 1048576 | tf_op jit(solution)/shard_map/all_to_all | solution.py:63
  18.1 45.4 %all-gather.27.cloned.1.call-start = ((), (), s32[]{:S(2)}) async-start(), calls=%async_computation.1 | async-start | bytes 2359296 | tf_op jit(solution)/shard_map/all_gather | solution.py:77
  35.3 30.6 %copy-start = (bf16[256,440]{1,0:T(8,128)(2,1)S(1)}, bf16[256,440]{1,0:T(8,128)(2,1)}, u32[]{:S(2)}) copy-start(bf16[256,440]{1,0:T(8,128)(2,1)} %gather_fusion.1) | copy-start | bytes 675844
  35.4 58.2 %all-gather.29.cloned.1.call-start = ((), (), s32[]{:S(2)}) async-start(), calls=%async_computation.2 | async-start | bytes 1310720 | tf_op jit(solution)/shard_map/all_gather | solution.py:15
  67.3 138.1 %all-gather.31.cloned.1.call-start = ((), (), s32[]{:S(2)}) async-start(), calls=%async_computation.3 | async-start | bytes 4718592 | tf_op jit(solution)/shard_map/all_gather | solution.py:15
  158.0 76.1 %all-gather.33.cloned.1.call-start = ((), (), s32[]{:S(2)}) async-start(), calls=%async_computation.4 | async-start | bytes 1310720 | tf_op jit(solution)/shard_map/all_gather | solution.py:15
  208.6 55.2 %all-gather.35.cloned.1.call-start = ((), (), s32[]{:S(2)}) async-start(), calls=%async_computation.5 | async-start | bytes 1310720 | tf_op jit(solution)/shard_map/all_gather | solution.py:15
  237.0 138.7 %all-gather.37.cloned.1.call-start = ((), (), s32[]{:S(2)}) async-start(), calls=%async_computation.6 | async-start | bytes 4718592 | tf_op jit(solution)/shard_map/all_gather | solution.py:15
  328.4 76.1 %all-gather.39.cloned.1.call-start = ((), (), s32[]{:S(2)}) async-start(), calls=%async_computation.7 | async-start | bytes 1310720 | tf_op jit(solution)/shard_map/all_gather | solution.py:15
  379.0 55.0 %all-gather.41.cloned.1.call-start = ((), (), s32[]{:S(2)}) async-start(), calls=%async_computation.8 | async-start | bytes 1310720 | tf_op jit(solution)/shard_map/all_gather | solution.py:15
  407.3 138.9 %all-gather.43.cloned.1.call-start = ((), (), s32[]{:S(2)}) async-start(), calls=%async_computation.9 | async-start | bytes 4718592 | tf_op jit(solution)/shard_map/all_gather | solution.py:15
  498.9 76.1 %all-gather.45.cloned.1.call-start = ((), (), s32[]{:S(2)}) async-start(), calls=%async_computation.10 | async-start | bytes 1310720 | tf_op jit(solution)/shard_map/all_gather | solution.py:15
  549.5 55.8 %all-gather.47.cloned.1.call-start = ((), (), s32[]{:S(2)}) async-start(), calls=%async_computation.11 | async-start | bytes 1310720 | tf_op jit(solution)/shard_map/all_gather | solution.py:15
  578.5 140.3 %all-gather.49.cloned.1.call-start = ((), (), s32[]{:S(2)}) async-start(), calls=%async_computation.12 | async-start | bytes 4718592 | tf_op jit(solution)/shard_map/all_gather | solution.py:15
  606.6 61.4 %copy-start.1 = (f32[256,512]{0,1:T(8,128)S(1)}, f32[256,512]{0,1:T(8,128)}, u32[]{:S(2)}) copy-start(f32[256,512]{0,1:T(8,128)} %get-tuple-element.120) | copy-start | bytes 1572868
  671.5 76.1 %all-gather.51.cloned.1.call-start = ((), (), s32[]{:S(2)}) async-start(), calls=%async_computation.13 | async-start | bytes 1310720 | tf_op jit(solution)/shard_map/all_gather | solution.py:15
Sparse Core Ops, SparseCore 0:
  35.5 27.9 all-gather.26
  67.4 26.1 all-gather.28
  158.1 47.1 all-gather.30
  208.7 25.3 all-gather.32
  237.1 26.6 all-gather.34
  328.5 47.1 all-gather.36
  379.1 25.3 all-gather.38
  407.4 26.6 all-gather.40
  499.0 47.1 all-gather.42
  549.6 25.3 all-gather.44
  578.6 26.6 all-gather.46
  671.7 47.1 all-gather.48
  722.2 25.3 all-gather.50
